TPU v7x, 256 devices: a whole 4x4x8 slice. The times are simulated.
256 devices in a mesh: ctx: 64 (over y, z_lo, x), tp: 4 (over z_hi, core).
Axes of the slice: x: 4, y: 4, z: 8 (z_hi: 2, z_lo: 4; z = z_hi * 4 + z_lo), core: 2. Of those that a mesh axis runs over, the one named last changes fastest.
Arguments:
- activations: bfloat16 [40960, 4096], P('ctx', 'tp'), may hold values from -6 to 6
- group_counts: int32 [64], replicated, may hold values from 1 to 5, as said below
- genome_starts: int32 [32], replicated, may hold values from 0 to 24448, as said below
- in_weight: bfloat16 [4096, 3, 2048], P('ctx', None, 'tp'), may hold values from -0.09375 to 0.09375
- short_taps: float32 [7, 3, 2048], P(None, None, 'tp'), may hold values from -2 to 2
- long_taps: float32 [128, 2048], P(None, 'tp'), may hold values from -0.5 to 0.5
- out_weight: bfloat16 [2048, 4096], P('tp', 'ctx'), may hold values from -0.125 to 0.125
Outputs:
- block_out: bfloat16 [40960, 4096], P('ctx', 'tp')
Inputs may be any that keep to these rules, and one draw needn't show every extreme that they name: Every device holds 1 or more blocks; group_counts[2k] + group_counts[2k+1] = 6 for every k. `genome_starts`: strictly increasing; the first entry is 0 and the last is exactly 24448.
All inputs are finite; a program needn't handle non-finite values.
Results may differ from a plain program's by a relative error of at most 0.012.
Values may be sent and summed in bfloat16 or wider, within the bound.
No kernel may reach another device: no remote copies, remote signals or barrier semaphores. Data moves between devices by JAX's collectives and lax.ppermute only.
A program may use at most 128 MiB of HBM per device.

v0:
```python
import jax
import jax.numpy as jnp
from jax import lax
from jax.sharding import PartitionSpec as P

GROUP = 128


def passed_along(shard, axis, by):
    peers = lax.axis_size(axis)
    pairs = [(i, i + by) for i in range(peers) if 0 <= i + by < peers]
    return lax.ppermute(shard, axis, pairs)


def genome_start(positions, genome_starts):
    above = genome_starts[None, :] <= positions[:, None]
    return jnp.max(jnp.where(above, genome_starts[None, :], 0), axis=1)


def causal_taps(padded, taps, positions, gstart, width):
    count = positions.shape[0]
    shape = (count,) + (1,) * (padded.ndim - 1)
    summed = jnp.zeros((count,) + padded.shape[1:], jnp.float32)
    for j in range(width):
        in_genome = (positions - j >= gstart).reshape(shape)
        window = padded[width - 1 - j : width - 1 - j + count]
        summed = summed + jnp.where(in_genome, window * taps[j], jnp.float32(0.0))
    return summed


def body(activations, group_counts, genome_starts, in_weight, short_taps, long_taps, out_weight):
    ctx_size = lax.axis_size("ctx")
    my_index = lax.axis_index("ctx")
    own_rows = activations.shape[0]
    device_ids = jnp.arange(ctx_size, dtype=jnp.int32)
    own_count = jnp.sum(jnp.where(device_ids == my_index, group_counts, 0))
    offset = jnp.sum(jnp.where(device_ids < my_index, group_counts, 0))
    row_ids = jnp.arange(own_rows, dtype=jnp.int32)
    positions = offset * GROUP + row_ids
    tail_end = own_count * GROUP

    def last_rows(source, count):
        return lax.dynamic_slice_in_dim(source, tail_end - count, count, 0)

    gstart = genome_start(positions, genome_starts)
    all_feats = lax.all_gather(activations, "tp", axis=1, tiled=True)
    widened = all_feats.astype(jnp.float32)
    normed = (
        widened * lax.rsqrt(jnp.mean(widened * widened, axis=1, keepdims=True) + 1e-06)
    ).astype(jnp.bfloat16)
    row_count = normed.shape[0]
    branches = in_weight.shape[1]
    chans = in_weight.shape[2]
    shard_rows = lax.all_gather(in_weight, "ctx", axis=0, tiled=True)
    flat = shard_rows.reshape(shard_rows.shape[0], branches * chans)
    summed = jnp.dot(normed, flat, preferred_element_type=jnp.float32)
    projected = summed.astype(jnp.bfloat16).reshape(row_count, branches, chans)
    rim_short = passed_along(last_rows(projected, 6), "ctx", 1)
    feat = causal_taps(
        jnp.concatenate([rim_short, projected], axis=0).astype(jnp.float32),
        short_taps,
        positions,
        gstart,
        7,
    )
    mixed = (feat[:, 1] * feat[:, 2]).astype(jnp.bfloat16)
    rim_long = passed_along(last_rows(mixed, 127), "ctx", 1)
    filtered = causal_taps(
        jnp.concatenate([rim_long, mixed], axis=0).astype(jnp.float32),
        long_taps,
        positions,
        gstart,
        128,
    )
    gated = (feat[:, 0] * filtered).astype(jnp.bfloat16)
    partial_out = jnp.dot(
        gated,
        lax.all_gather(out_weight, "ctx", axis=1, tiled=True),
        preferred_element_type=jnp.float32,
    )
    branch_out = lax.psum_scatter(
        partial_out.astype(jnp.bfloat16), "tp", scatter_dimension=1, tiled=True
    ).astype(jnp.float32)
    result = (activations.astype(jnp.float32) + branch_out).astype(jnp.bfloat16)
    slot_ids = jnp.arange(own_rows, dtype=jnp.int32)
    live_rows = (slot_ids < own_count * GROUP)[:, None]
    return jnp.where(live_rows, result, jnp.zeros_like(result))


def solution(mesh):
    placed = (
        P("ctx", "tp"),
        P(),
        P(),
        P("ctx", None, "tp"),
        P(None, None, "tp"),
        P(None, "tp"),
        P("tp", "ctx"),
    )
    return jax.shard_map(
        body, mesh=mesh, in_specs=placed, out_specs=P("ctx", "tp"), check_vma=False
    )
```

profile of v0, /device:TPU:1, one launch (start us, length us, event | category | flops | bytes accessed | tf_op | source)
XLA Modules:
  0.0 921.4 jit_solution(7368510152280378375)
XLA Ops:
  6.5 0.0 all-gather.4.cloned.1.call-start
  6.6 0.7 all-gather.4.cloned.1.call-update
  7.3 0.0 all-gather.6.cloned.1.call-start
  7.3 0.7 all-gather.6.cloned.1.call-update
  8.0 0.0 all-gather.8.cloned.1.call-start
  8.1 0.7 all-gather.8.cloned.1.call-update
  8.8 0.0 reduce-scatter.2.cloned.1.call-start
  8.8 0.0 copy-done.1
  9.1 0.0 copy-done.44
  9.1 0.6 fusion.283
  11.0 0.0 copy-done.2
  11.1 0.0 copy-done.43
  11.1 0.1 select_reduce_fusion
  11.2 1.3 add_compare_fusion.95
  12.5 79.1 %all-gather.4.cloned.1.call-done = bf16[640,4096]{1,0:T(8,128)(2,1)} async-done(((bf16[640,1024]{1,0:T(8,128)(2,1)}), bf16[640,4096]{1,0:T(8,128)(2,1)}) %all-gather.4.cloned.1.call-update) | async-done | bytes 5242896 | tf_op jit(solution)/shard_map/all_gather | solution.py:46
  91.6 3.6 fusion
  95.2 321.5 %all-gather.6.cloned.1.call-done = bf16[4096,3,512]{2,0,1:T(8,128)(2,1)} async-done(((bf16[64,3,512]{2,0,1:T(8,128)(2,1)}), bf16[4096,3,512]{2,0,1:T(8,128)(2,1)}) %all-gather.6.cloned.1.call-update) | async-done | bytes 12582928 | tf_op jit(solution)/shard_map/all_gather | solution.py:54
  416.7 17.0 %copy.21 = bf16[4096,3,512]{0,2,1:T(8,128)(2,1)} copy(bf16[4096,3,512]{2,0,1:T(8,128)(2,1)} %all-gather.6.cloned.1.call-done) | data formatting | bytes 25165824 | tf_op jit(solution)/shard_map/all_gather | solution.py:54
  433.7 13.9 %fusion.18 = bf16[640,1536]{1,0:T(8,128)(2,1)} fusion(bf16[4096,1536]{0,1:T(8,128)(2,1)} %bitcast.161, bf16[640,4096]{1,0:T(8,128)(2,1)} %all-gather.4.cloned.1.call-done, f32[640]{0:T(1024)S(1)} %add_rsqrt_fusion), kind=kOutput, calls=%fused_computation.27 | convolution fusion | flops 8061911040 | bytes 19794432 | tf_op jit(solution)/shard_map/dot_general | solution.py:56
  447.6 2.8 copy.22
  450.4 0.2 constant_dynamic-slice_fusion
  450.6 1.3 collective-permute-start
  451.9 5.6 collective-permute-done
  457.5 1.0 maximum_convert_fusion
  458.6 8.1 fusion.6
  466.7 0.1 fusion.279
  466.8 0.1 dynamic-slice_bitcast_fusion
  466.9 4.0 collective-permute-start.1
  470.9 0.1 fusion.295
  471.0 1.9 collective-permute-done.1
  473.0 0.4 maximum_convert_fusion.1
  473.3 0.0 copy-start.3
  473.4 0.0 copy-start.4
  473.4 0.0 copy-start.5
  473.4 0.0 copy-start.6
  473.4 0.0 copy-start.7
  473.4 0.0 copy-start.8
  473.4 0.0 copy-start.9
  473.4 0.0 copy-start.10
  473.4 0.0 copy-start.11
  473.4 0.0 copy-start.12
  473.5 0.0 copy-start.13
  473.5 0.0 copy-start.14
  473.5 0.0 copy-start.15
  473.5 0.0 copy-start.16
  473.5 0.0 copy-start.17
  473.5 0.0 copy-start.18
  473.5 0.0 copy-start.19
  473.5 0.0 copy-start.20
  473.5 0.0 copy-start.21
  473.5 0.0 copy-start.22
  473.6 0.0 copy-start.23
  473.6 0.0 copy-start.24
  473.6 0.0 copy-start.25
  473.6 0.0 copy-start.26
  473.6 0.0 copy-start.27
  473.8 15.7 %fusion.217 = f32[640,512]{0,1:T(8,128)S(1)} fusion(f32[767,512]{0,1:T(8,128)S(1)} %maximum_convert_fusion.1, f32[512]{0:T(512)S(1)} %bitcast.178, f32[512]{0:T(512)S(1)} %bitcast.179, f32[512]{0:T(512)S(1)} %bitcast.180, f32[512]{0:T(512)S(1)} %bitcast.181, f32[512]{0:T(512)S(1)} %bitcast.182, f32[512]{0:T(512)S(1)} %bitcast.183, f32[512]{0:T(512)S(1)} %bitcast.184, ...), kind=kLoop, calls=%fused_computation.323 | loop fusion | flops 31129600 | bytes 43339776 | tf_op jit(solution)/shard_map/add | solution.py:27
  489.9 47.7 %fusion.299 = bf16[640,512]{0,1:T(8,128)(2,1)S(1)} fusion(f32[767,512]{0,1:T(8,128)S(1)} %maximum_convert_fusion.1, f32[640,512]{0,1:T(8,128)S(1)} %fusion.217, f32[512]{0:T(512)S(1)} %bitcast.197, f32[512]{0:T(512)S(1)} %bitcast.292, f32[512]{0:T(512)S(1)} %bitcast.237, f32[512]{0:T(512)S(1)} %bitcast.238, f32[512]{0:T(512)S(1)} %bitcast.239, ...), kind=kLoop, calls=%fused_computation.35.clone.clone.1 | loop fusion | flops 95027200 | bytes 129363968 | tf_op jit(solution)/shard_map/dot_general | solution.py:76
  537.6 228.4 %all-gather.8.cloned.1.call-done = bf16[512,4096]{0,1:T(8,128)(2,1)} async-done(((bf16[512,64]{0,1:T(8,128)(2,1)}), bf16[512,4096]{0,1:T(8,128)(2,1)}) %all-gather.8.cloned.1.call-update) | async-done | bytes 4194320 | tf_op jit(solution)/shard_map/all_gather | solution.py:78
  766.1 7.5 convolution_convert_fusion
  773.5 0.0 reduce-scatter.2.cloned.1.call-update
  773.6 138.5 %reduce-scatter.2.cloned.1.call-done = bf16[640,1024]{1,0:T(8,128)(2,1)} async-done(((bf16[640,4096]{1,0:T(8,128)(2,1)}), bf16[640,1024]{1,0:T(8,128)(2,1)}) %reduce-scatter.2.cloned.1.call-update) | async-done | bytes 1310736 | tf_op jit(solution)/shard_map/reduce_scatter | solution.py:81
  912.0 0.0 copy-done
  912.0 2.8 fusion.21
  (75 shorter events, 0.4 us)
Async XLA Ops:
  6.5 2.3 copy-start.1
  6.5 2.6 copy-start.44
  6.5 4.5 copy-start.2
  6.5 4.5 copy-start.43
  6.5 85.1 %all-gather.4.cloned.1.call-start = ((), (), s32[]{:S(2)}) async-start(), calls=%async_computation.1 | async-start | bytes 6553600 | tf_op jit(solution)/shard_map/all_gather | solution.py:46
  7.3 409.5 %all-gather.6.cloned.1.call-start = ((), (), s32[]{:S(2)}) async-start(), calls=%async_computation.2 | async-start | bytes 12779520 | tf_op jit(solution)/shard_map/all_gather | solution.py:54
  8.0 758.1 %all-gather.8.cloned.1.call-start = ((), (), s32[]{:S(2)}) async-start(), calls=%async_computation.3 | async-start | bytes 4259840 | tf_op jit(solution)/shard_map/all_gather | solution.py:78
  8.8 903.3 %reduce-scatter.2.cloned.1.call-start = ((), (), s32[]{:S(2)}) async-start(), calls=%async_computation.4 | async-start | bytes 6553600 | tf_op jit(solution)/shard_map/reduce_scatter | solution.py:81
  450.6 7.0 collective-permute-start
  466.9 6.1 collective-permute-start.1
  473.3 16.1 %copy-start.3 = (pred[640]{0:T(1024)(128)(4,1)S(1)}, pred[640]{0:T(1024)(128)(4,1)}, u32[]{:S(2)}) copy-start(pred[640]{0:T(1024)(128)(4,1)} %get-tuple-element.160) | copy-start | bytes 1924
  473.4 16.1 %copy-start.4 = (pred[640]{0:T(1024)(128)(4,1)S(1)}, pred[640]{0:T(1024)(128)(4,1)}, u32[]{:S(2)}) copy-start(pred[640]{0:T(1024)(128)(4,1)} %get-tuple-element.161) | copy-start | bytes 1924
  473.4 16.1 %copy-start.5 = (pred[640]{0:T(1024)(128)(4,1)S(1)}, pred[640]{0:T(1024)(128)(4,1)}, u32[]{:S(2)}) copy-start(pred[640]{0:T(1024)(128)(4,1)} %get-tuple-element.162) | copy-start | bytes 1924
  473.4 16.1 %copy-start.6 = (pred[640]{0:T(1024)(128)(4,1)S(1)}, pred[640]{0:T(1024)(128)(4,1)}, u32[]{:S(2)}) copy-start(pred[640]{0:T(1024)(128)(4,1)} %get-tuple-element.163) | copy-start | bytes 1924
  473.4 16.1 %copy-start.7 = (pred[640]{0:T(1024)(128)(4,1)S(1)}, pred[640]{0:T(1024)(128)(4,1)}, u32[]{:S(2)}) copy-start(pred[640]{0:T(1024)(128)(4,1)} %get-tuple-element.164) | copy-start | bytes 1924
  473.4 16.1 %copy-start.8 = (pred[640]{0:T(1024)(128)(4,1)S(1)}, pred[640]{0:T(1024)(128)(4,1)}, u32[]{:S(2)}) copy-start(pred[640]{0:T(1024)(128)(4,1)} %get-tuple-element.165) | copy-start | bytes 1924
  473.4 16.1 %copy-start.9 = (pred[640]{0:T(1024)(128)(4,1)S(1)}, pred[640]{0:T(1024)(128)(4,1)}, u32[]{:S(2)}) copy-start(pred[640]{0:T(1024)(128)(4,1)} %get-tuple-element.166) | copy-start | bytes 1924
  473.4 16.1 %copy-start.10 = (pred[640]{0:T(1024)(128)(4,1)S(1)}, pred[640]{0:T(1024)(128)(4,1)}, u32[]{:S(2)}) copy-start(pred[640]{0:T(1024)(128)(4,1)} %get-tuple-element.167) | copy-start | bytes 1924
  473.4 16.1 %copy-start.11 = (pred[640]{0:T(1024)(128)(4,1)S(1)}, pred[640]{0:T(1024)(128)(4,1)}, u32[]{:S(2)}) copy-start(pred[640]{0:T(1024)(128)(4,1)} %get-tuple-element.168) | copy-start | bytes 1924
  473.4 16.1 %copy-start.12 = (pred[640]{0:T(1024)(128)(4,1)S(1)}, pred[640]{0:T(1024)(128)(4,1)}, u32[]{:S(2)}) copy-start(pred[640]{0:T(1024)(128)(4,1)} %get-tuple-element.169) | copy-start | bytes 1924
  473.5 16.1 %copy-start.13 = (pred[640]{0:T(1024)(128)(4,1)S(1)}, pred[640]{0:T(1024)(128)(4,1)}, u32[]{:S(2)}) copy-start(pred[640]{0:T(1024)(128)(4,1)} %get-tuple-element.170) | copy-start | bytes 1924
  473.5 16.1 %copy-start.14 = (pred[640]{0:T(1024)(128)(4,1)S(1)}, pred[640]{0:T(1024)(128)(4,1)}, u32[]{:S(2)}) copy-start(pred[640]{0:T(1024)(128)(4,1)} %get-tuple-element.171) | copy-start | bytes 1924
  473.5 16.1 %copy-start.15 = (pred[640]{0:T(1024)(128)(4,1)S(1)}, pred[640]{0:T(1024)(128)(4,1)}, u32[]{:S(2)}) copy-start(pred[640]{0:T(1024)(128)(4,1)} %get-tuple-element.172) | copy-start | bytes 1924
  473.5 16.1 %copy-start.16 = (pred[640]{0:T(1024)(128)(4,1)S(1)}, pred[640]{0:T(1024)(128)(4,1)}, u32[]{:S(2)}) copy-start(pred[640]{0:T(1024)(128)(4,1)} %get-tuple-element.173) | copy-start | bytes 1924
  473.5 16.1 %copy-start.17 = (pred[640]{0:T(1024)(128)(4,1)S(1)}, pred[640]{0:T(1024)(128)(4,1)}, u32[]{:S(2)}) copy-start(pred[640]{0:T(1024)(128)(4,1)} %get-tuple-element.174) | copy-start | bytes 1924
  473.5 16.1 %copy-start.18 = (pred[640]{0:T(1024)(128)(4,1)S(1)}, pred[640]{0:T(1024)(128)(4,1)}, u32[]{:S(2)}) copy-start(pred[640]{0:T(1024)(128)(4,1)} %get-tuple-element.175) | copy-start | bytes 1924
  473.5 16.1 %copy-start.19 = (pred[640]{0:T(1024)(128)(4,1)S(1)}, pred[640]{0:T(1024)(128)(4,1)}, u32[]{:S(2)}) copy-start(pred[640]{0:T(1024)(128)(4,1)} %get-tuple-element.176) | copy-start | bytes 1924
  473.5 16.1 %copy-start.20 = (pred[640]{0:T(1024)(128)(4,1)S(1)}, pred[640]{0:T(1024)(128)(4,1)}, u32[]{:S(2)}) copy-start(pred[640]{0:T(1024)(128)(4,1)} %get-tuple-element.177) | copy-start | bytes 1924
  473.5 16.1 %copy-start.21 = (pred[640]{0:T(1024)(128)(4,1)S(1)}, pred[640]{0:T(1024)(128)(4,1)}, u32[]{:S(2)}) copy-start(pred[640]{0:T(1024)(128)(4,1)} %get-tuple-element.178) | copy-start | bytes 1924
  473.5 16.1 %copy-start.22 = (pred[640]{0:T(1024)(128)(4,1)S(1)}, pred[640]{0:T(1024)(128)(4,1)}, u32[]{:S(2)}) copy-start(pred[640]{0:T(1024)(128)(4,1)} %get-tuple-element.179) | copy-start | bytes 1924
  473.6 16.1 %copy-start.23 = (pred[640]{0:T(1024)(128)(4,1)S(1)}, pred[640]{0:T(1024)(128)(4,1)}, u32[]{:S(2)}) copy-start(pred[640]{0:T(1024)(128)(4,1)} %get-tuple-element.180) | copy-start | bytes 1924
  473.6 16.1 %copy-start.24 = (pred[640]{0:T(1024)(128)(4,1)S(1)}, pred[640]{0:T(1024)(128)(4,1)}, u32[]{:S(2)}) copy-start(pred[640]{0:T(1024)(128)(4,1)} %get-tuple-element.181) | copy-start | bytes 1924
  473.6 16.1 %copy-start.25 = (pred[640]{0:T(1024)(128)(4,1)S(1)}, pred[640]{0:T(1024)(128)(4,1)}, u32[]{:S(2)}) copy-start(pred[640]{0:T(1024)(128)(4,1)} %get-tuple-element.182) | copy-start | bytes 1924
  473.6 16.1 %copy-start.26 = (pred[640]{0:T(1024)(128)(4,1)S(1)}, pred[640]{0:T(1024)(128)(4,1)}, u32[]{:S(2)}) copy-start(pred[640]{0:T(1024)(128)(4,1)} %get-tuple-element.183) | copy-start | bytes 1924
  473.6 16.1 %copy-start.27 = (pred[640]{0:T(1024)(128)(4,1)S(1)}, pred[640]{0:T(1024)(128)(4,1)}, u32[]{:S(2)}) copy-start(pred[640]{0:T(1024)(128)(4,1)} %get-tuple-element.184) | copy-start | bytes 1924
  473.6 16.1 %copy-start.28 = (pred[640]{0:T(1024)(128)(4,1)S(1)}, pred[640]{0:T(1024)(128)(4,1)}, u32[]{:S(2)}) copy-start(pred[640]{0:T(1024)(128)(4,1)} %get-tuple-element.185) | copy-start | bytes 1924
  473.6 16.1 %copy-start.29 = (pred[640]{0:T(1024)(128)(4,1)S(1)}, pred[640]{0:T(1024)(128)(4,1)}, u32[]{:S(2)}) copy-start(pred[640]{0:T(1024)(128)(4,1)} %get-tuple-element.186) | copy-start | bytes 1924
  473.6 16.1 %copy-start.30 = (pred[640]{0:T(1024)(128)(4,1)S(1)}, pred[640]{0:T(1024)(128)(4,1)}, u32[]{:S(2)}) copy-start(pred[640]{0:T(1024)(128)(4,1)} %get-tuple-element.187) | copy-start | bytes 1924
  473.6 16.1 %copy-start.31 = (pred[640]{0:T(1024)(128)(4,1)S(1)}, pred[640]{0:T(1024)(128)(4,1)}, u32[]{:S(2)}) copy-start(pred[640]{0:T(1024)(128)(4,1)} %get-tuple-element.188) | copy-start | bytes 1924
  473.6 16.1 %copy-start.32 = (pred[640]{0:T(1024)(128)(4,1)S(1)}, pred[640]{0:T(1024)(128)(4,1)}, u32[]{:S(2)}) copy-start(pred[640]{0:T(1024)(128)(4,1)} %get-tuple-element.189) | copy-start | bytes 1924
  473.7 16.1 %copy-start.33 = (pred[640]{0:T(1024)(128)(4,1)S(1)}, pred[640]{0:T(1024)(128)(4,1)}, u32[]{:S(2)}) copy-start(pred[640]{0:T(1024)(128)(4,1)} %get-tuple-element.190) | copy-start | bytes 1924
  473.7 16.1 %copy-start.34 = (pred[640]{0:T(1024)(128)(4,1)S(1)}, pred[640]{0:T(1024)(128)(4,1)}, u32[]{:S(2)}) copy-start(pred[640]{0:T(1024)(128)(4,1)} %get-tuple-element.191) | copy-start | bytes 1924
  473.7 16.1 %copy-start.35 = (pred[640]{0:T(1024)(128)(4,1)S(1)}, pred[640]{0:T(1024)(128)(4,1)}, u32[]{:S(2)}) copy-start(pred[640]{0:T(1024)(128)(4,1)} %get-tuple-element.192) | copy-start | bytes 1924
  473.7 16.1 %copy-start.36 = (pred[640]{0:T(1024)(128)(4,1)S(1)}, pred[640]{0:T(1024)(128)(4,1)}, u32[]{:S(2)}) copy-start(pred[640]{0:T(1024)(128)(4,1)} %get-tuple-element.193) | copy-start | bytes 1924
  473.7 16.1 %copy-start.37 = (pred[640]{0:T(1024)(128)(4,1)S(1)}, pred[640]{0:T(1024)(128)(4,1)}, u32[]{:S(2)}) copy-start(pred[640]{0:T(1024)(128)(4,1)} %get-tuple-element.194) | copy-start | bytes 1924
  473.7 16.1 %copy-start.38 = (pred[640]{0:T(1024)(128)(4,1)S(1)}, pred[640]{0:T(1024)(128)(4,1)}, u32[]{:S(2)}) copy-start(pred[640]{0:T(1024)(128)(4,1)} %get-tuple-element.195) | copy-start | bytes 1924
  473.7 16.1 %copy-start.39 = (pred[640]{0:T(1024)(128)(4,1)S(1)}, pred[640]{0:T(1024)(128)(4,1)}, u32[]{:S(2)}) copy-start(pred[640]{0:T(1024)(128)(4,1)} %get-tuple-element.196) | copy-start | bytes 1924
  473.7 16.1 %copy-start.40 = (pred[640]{0:T(1024)(128)(4,1)S(1)}, pred[640]{0:T(1024)(128)(4,1)}, u32[]{:S(2)}) copy-start(pred[640]{0:T(1024)(128)(4,1)} %get-tuple-element.197) | copy-start | bytes 1924
  473.7 16.1 %copy-start.41 = (pred[640]{0:T(1024)(128)(4,1)S(1)}, pred[640]{0:T(1024)(128)(4,1)}, u32[]{:S(2)}) copy-start(pred[640]{0:T(1024)(128)(4,1)} %get-tuple-element.198) | copy-start | bytes 1924
  473.7 16.1 %copy-start.42 = (pred[640]{0:T(1024)(128)(4,1)S(1)}, pred[640]{0:T(1024)(128)(4,1)}, u32[]{:S(2)}) copy-start(pred[640]{0:T(1024)(128)(4,1)} %get-tuple-element.199) | copy-start | bytes 1924
  773.5 138.5 %copy-start = (bf16[640,1024]{1,0:T(8,128)(2,1)S(1)}, bf16[640,1024]{1,0:T(8,128)(2,1)}, u32[]{:S(2)}) copy-start(bf16[640,1024]{1,0:T(8,128)(2,1)} %param.7) | copy-start | bytes 3932164
Sparse Core Ops, SparseCore 0:
  9.2 82.4 all-gather.3
  93.4 323.2 all-gather.5
  418.5 347.5 all-gather.7
  773.7 138.3 reduce-scatter.1
where the time goes:
time: 922 us; the launch traced here: 921 us
  waiting for transfers between devices  777 us (84%)
  other arithmetic  81.6 us (9%)
  matrix products  21.4 us (2%)
  local copies, waits for them, and re-layouts  20.5 us (2%)
  between operations  15.3 us (2%)
    all_gather x1, waiting for transfers between devices, body(): shard_rows = lax.all_gather(in_weight, 'ctx', axis=0, tiled=True)  322 us
    all_gather x1, waiting for transfers between devices, body(): lax.all_gather(out_weight, 'ctx', axis=1, tiled=True)  228 us
    reduce_scatter x1, waiting for transfers between devices, body(): lax.psum_scatter(partial_out.astype(jnp.bfloat16), 'tp', scatter_dimensio...  138 us
    all_gather x1, waiting for transfers between devices, body(): all_feats = lax.all_gather(activations, 'tp', axis=1, tiled=True)  79.1 us
    dot_general x1, other arithmetic, body(): jnp.dot(gated, lax.all_gather(out_weight, 'ctx', axis=1, tiled=True), pre...  47.7 us
    add x2, other arithmetic, causal_taps(): summed = summed + jnp.where(in_genome, window * taps[j], jnp.float32(0.0))  23.8 us
  transfers between devices with their start and end apart: 6, of which 6 were waited for; matrix products, arithmetic and copies ran while one was open for 12% of the time, Pallas kernels for 0%

commit v1 on v0

--- a/solution.py
+++ b/solution.py
@@ -43,7 +43,15 @@
         return lax.dynamic_slice_in_dim(source, tail_end - count, count, 0)
 
     gstart = genome_start(positions, genome_starts)
-    all_feats = lax.all_gather(activations, "tp", axis=1, tiled=True)
+    all_feats = jnp.concatenate(
+        lax.all_to_all(
+            jnp.stack([activations for _ in range(lax.psum(1, "tp"))]),
+            axis_name="tp",
+            concat_axis=0,
+            split_axis=0,
+        ),
+        1,
+    )
     widened = all_feats.astype(jnp.float32)
     normed = (
         widened * lax.rsqrt(jnp.mean(widened * widened, axis=1, keepdims=True) + 1e-06)

time: 922 us -> 887 us (0.962)
  waiting for transfers between devices: 777 us -> 722 us
  starting transfers between devices: 5.46 us -> 15.4 us
    all_to_all x0 -> x1, waiting for transfers between devices: none -> 157 us  [body(): lax.all_to_all(jnp.stack([activations for _ in range(lax.psum(1, 'tp'))])...]
    all_gather x1, waiting for transfers between devices: 322 us -> 200 us  [body(): shard_rows = lax.all_gather(in_weight, 'ctx', axis=0, tiled=True)]
    all_gather x1 -> x0, waiting for transfers between devices: 79.1 us -> none  [body(): all_feats = lax.all_gather(activations, 'tp', axis=1, tiled=True)]
    all_to_all x0 -> x1, starting transfers between devices: none -> 10.1 us  [body(): lax.all_to_all(jnp.stack([activations for _ in range(lax.psum(1, 'tp'))])...]
    all_gather x1, waiting for transfers between devices: 228 us -> 219 us  [body(): lax.all_gather(out_weight, 'ctx', axis=1, tiled=True)]
  transfers between devices with their start and end apart: 6 -> 6, of which waited for: 6 -> 6; matrix products, arithmetic and copies ran while one was open for 12% -> 14% of each run, Pallas kernels for 0% -> 0%
where the time goes in v1:
time: 887 us; the launch traced here: 886 us
  waiting for transfers between devices  722 us (81%)
  other arithmetic  87.5 us (10%)
  local copies, waits for them, and re-layouts  24.9 us (3%)
  matrix products  21.3 us (2%)
  starting transfers between devices  15.4 us (2%)
  between operations  15.2 us (2%)
    all_gather x1, waiting for transfers between devices, body(): lax.all_gather(out_weight, 'ctx', axis=1, tiled=True)  219 us
    all_gather x1, waiting for transfers between devices, body(): shard_rows = lax.all_gather(in_weight, 'ctx', axis=0, tiled=True)  200 us
    all_to_all x1, waiting for transfers between devices, body(): lax.all_to_all(jnp.stack([activations for _ in range(lax.psum(1, 'tp'))])...  157 us
    reduce_scatter x1, waiting for transfers between devices, body(): lax.psum_scatter(partial_out.astype(jnp.bfloat16), 'tp', scatter_dimensio...  138 us
    dot_general x1, other arithmetic, body(): jnp.dot(gated, lax.all_gather(out_weight, 'ctx', axis=1, tiled=True), pre...  47.7 us
    add x2, other arithmetic, causal_taps(): summed = summed + jnp.where(in_genome, window * taps[j], jnp.float32(0.0))  23.8 us
  transfers between devices with their start and end apart: 6, of which 6 were waited for; matrix products, arithmetic and copies ran while one was open for 14% of the time, Pallas kernels for 0%

profile of v1, /device:TPU:1, one launch (start us, length us, event | category | flops | bytes accessed | tf_op | source)
XLA Modules:
  0.0 886.5 jit_solution(1127656682145032444)
XLA Ops:
  6.5 0.0 all-gather.3.cloned.1.call-start
  6.5 0.7 all-gather.3.cloned.1.call-update
  7.3 1.7 copy.23
  9.0 2.8 stack.2
  11.8 10.1 %all-to-all-start = ((bf16[4,640,1024]{1,2,0:T(8,128)(2,1)}), bf16[4,640,1024]{1,2,0:T(8,128)(2,1)}, u32[]{:S(2)}, u32[]{:S(2)}) async-start(bf16[4,640,1024]{1,2,0:T(8,128)(2,1)} %stack.2), calls=%async_computation | async-start | bytes 10485760 | tf_op jit(solution)/shard_map/all_to_all | solution.py:47
  21.8 0.0 all-gather.5.cloned.1.call-start
  21.9 0.7 all-gather.5.cloned.1.call-update
  22.6 0.0 reduce-scatter.2.cloned.1.call-start
  22.6 0.0 copy-done.44
  22.6 0.6 fusion.277
  24.5 0.0 copy-done.43
  24.5 0.1 select_reduce_fusion
  24.6 0.0 copy-done.2
  24.7 0.0 copy-done.1
  25.0 1.3 add_compare_fusion.95
  26.3 157.1 %all-to-all-done = bf16[4,640,1024]{1,2,0:T(8,128)(2,1)} async-done(((bf16[4,640,1024]{1,2,0:T(8,128)(2,1)}), bf16[4,640,1024]{1,2,0:T(8,128)(2,1)}, u32[]{:S(2)}, u32[]{:S(2)}) %all-to-all-start) | async-done | bytes 5242912 | tf_op jit(solution)/shard_map/all_to_all | solution.py:47
  183.4 3.6 fusion
  187.0 5.9 fusion.1
  192.8 200.0 %all-gather.3.cloned.1.call-done = bf16[4096,3,512]{2,0,1:T(8,128)(2,1)} async-done(((bf16[64,3,512]{2,0,1:T(8,128)(2,1)}), bf16[4096,3,512]{2,0,1:T(8,128)(2,1)}) %all-gather.3.cloned.1.call-update) | async-done | bytes 12582928 | tf_op jit(solution)/shard_map/all_gather | solution.py:62
  392.8 16.9 %copy.24 = bf16[4096,3,512]{0,2,1:T(8,128)(2,1)} copy(bf16[4096,3,512]{2,0,1:T(8,128)(2,1)} %all-gather.3.cloned.1.call-done) | data formatting | bytes 25165824 | tf_op jit(solution)/shard_map/all_gather | solution.py:62
  409.8 13.9 %convolution_convert_fusion.1 = bf16[640,1536]{1,0:T(8,128)(2,1)} fusion(bf16[640,4096]{0,1:T(8,128)(2,1)} %bitcast.168, bf16[4096,1536]{0,1:T(8,128)(2,1)} %bitcast.165), kind=kOutput, calls=%fused_computation.25 | convolution fusion | flops 8054046720 | bytes 19791872 | tf_op jit(solution)/shard_map/dot_general | solution.py:64
  423.7 2.8 copy.25
  426.4 0.2 constant_dynamic-slice_fusion
  426.6 1.5 collective-permute-start
  428.2 4.5 collective-permute-done
  432.6 1.0 maximum_convert_fusion
  433.7 8.1 fusion.3
  441.7 0.1 fusion.273
  441.9 0.1 dynamic-slice_bitcast_fusion
  442.0 3.8 collective-permute-start.1
  445.8 0.1 fusion.290
  445.9 2.2 collective-permute-done.1
  448.2 0.4 maximum_convert_fusion.1
  448.6 0.0 copy-start.3
  448.6 0.0 copy-start.4
  448.6 0.0 copy-start.5
  448.6 0.0 copy-start.6
  448.6 0.0 copy-start.7
  448.6 0.0 copy-start.8
  448.6 0.0 copy-start.9
  448.6 0.0 copy-start.10
  448.6 0.0 copy-start.11
  448.7 0.0 copy-start.12
  448.7 0.0 copy-start.13
  448.7 0.0 copy-start.14
  448.7 0.0 copy-start.15
  448.7 0.0 copy-start.16
  448.7 0.0 copy-start.17
  448.7 0.0 copy-start.18
  448.7 0.0 copy-start.19
  448.7 0.0 copy-start.20
  448.7 0.0 copy-start.21
  448.8 0.0 copy-start.22
  448.8 0.0 copy-start.23
  448.8 0.0 copy-start.24
  448.8 0.0 copy-start.25
  448.8 0.0 copy-start.26
  449.0 15.7 %fusion.211 = f32[640,512]{0,1:T(8,128)S(1)} fusion(f32[767,512]{0,1:T(8,128)S(1)} %maximum_convert_fusion.1, f32[512]{0:T(512)S(1)} %bitcast.183, f32[512]{0:T(512)S(1)} %bitcast.184, f32[512]{0:T(512)S(1)} %bitcast.185, f32[512]{0:T(512)S(1)} %bitcast.186, f32[512]{0:T(512)S(1)} %bitcast.187, f32[512]{0:T(512)S(1)} %bitcast.188, f32[512]{0:T(512)S(1)} %bitcast.189, ...), kind=kLoop, calls=%fused_computation.321 | loop fusion | flops 31129600 | bytes 43339776 | tf_op jit(solution)/shard_map/add | solution.py:27
  465.1 47.7 %fusion.294 = bf16[640,512]{0,1:T(8,128)(2,1)S(1)} fusion(f32[767,512]{0,1:T(8,128)S(1)} %maximum_convert_fusion.1, f32[640,512]{0,1:T(8,128)S(1)} %fusion.211, f32[512]{0:T(512)S(1)} %bitcast.202, f32[512]{0:T(512)S(1)} %bitcast.297, f32[512]{0:T(512)S(1)} %bitcast.242, f32[512]{0:T(512)S(1)} %bitcast.243, f32[512]{0:T(512)S(1)} %bitcast.244, ...), kind=kLoop, calls=%fused_computation.33.clone.clone.1 | loop fusion | flops 95027200 | bytes 129363968 | tf_op jit(solution)/shard_map/dot_general | solution.py:84
  512.9 218.5 %all-gather.5.cloned.1.call-done = bf16[512,4096]{0,1:T(8,128)(2,1)} async-done(((bf16[512,64]{0,1:T(8,128)(2,1)}), bf16[512,4096]{0,1:T(8,128)(2,1)}) %all-gather.5.cloned.1.call-update) | async-done | bytes 4194320 | tf_op jit(solution)/shard_map/all_gather | solution.py:86
  731.4 7.5 convolution_convert_fusion
  738.9 0.0 reduce-scatter.2.cloned.1.call-update
  738.9 138.3 %reduce-scatter.2.cloned.1.call-done = bf16[640,1024]{1,0:T(8,128)(2,1)} async-done(((bf16[640,4096]{1,0:T(8,128)(2,1)}), bf16[640,1024]{1,0:T(8,128)(2,1)}) %reduce-scatter.2.cloned.1.call-update) | async-done | bytes 1310736 | tf_op jit(solution)/shard_map/reduce_scatter | solution.py:89
  877.2 2.8 fusion.15
  (77 shorter events, 0.4 us)
Async XLA Ops:
  6.5 386.3 %all-gather.3.cloned.1.call-start = ((), (), s32[]{:S(2)}) async-start(), calls=%async_computation.2 | async-start | bytes 12779520 | tf_op jit(solution)/shard_map/all_gather | solution.py:62
  11.7 10.9 %copy-start.44 = (s32[64]{0:T(128)S(1)}, s32[64]{0:T(128)}, u32[]{:S(2)}) copy-start(s32[64]{0:T(128)} %param.8) | copy-start | bytes 772
  11.7 12.8 %copy-start.43 = (s32[32]{0:T(128)S(1)}, s32[32]{0:T(128)}, u32[]{:S(2)}) copy-start(s32[32]{0:T(128)} %param.9) | copy-start | bytes 388
  11.8 12.9 %copy-start.2 = (f32[7,3,512]{2,0,1:T(8,128)S(1)}, f32[7,3,512]{2,0,1:T(8,128)}, u32[]{:S(2)}) copy-start(f32[7,3,512]{2,0,1:T(8,128)} %param.11) | copy-start | bytes 129028
  11.8 12.9 %copy-start.1 = (f32[128,512]{1,0:T(8,128)S(1)}, f32[128,512]{1,0:T(8,128)}, u32[]{:S(2)}) copy-start(f32[128,512]{1,0:T(8,128)} %param.12) | copy-start | bytes 786436
  11.8 171.6 %all-to-all-start = ((bf16[4,640,1024]{1,2,0:T(8,128)(2,1)}), bf16[4,640,1024]{1,2,0:T(8,128)(2,1)}, u32[]{:S(2)}, u32[]{:S(2)}) async-start(bf16[4,640,1024]{1,2,0:T(8,128)(2,1)} %stack.2), calls=%async_computation | async-start | bytes 10485760 | tf_op jit(solution)/shard_map/all_to_all | solution.py:47
  21.8 709.5 %all-gather.5.cloned.1.call-start = ((), (), s32[]{:S(2)}) async-start(), calls=%async_computation.3 | async-start | bytes 4259840 | tf_op jit(solution)/shard_map/all_gather | solution.py:86
  22.6 854.6 %reduce-scatter.2.cloned.1.call-start = ((), (), s32[]{:S(2)}) async-start(), calls=%async_computation.4 | async-start | bytes 6553600 | tf_op jit(solution)/shard_map/reduce_scatter | solution.py:89
  426.6 6.0 collective-permute-start
  442.0 6.2 collective-permute-start.1
  448.6 16.1 %copy-start.3 = (pred[640]{0:T(1024)(128)(4,1)S(1)}, pred[640]{0:T(1024)(128)(4,1)}, u32[]{:S(2)}) copy-start(pred[640]{0:T(1024)(128)(4,1)} %get-tuple-element.160) | copy-start | bytes 1924
  448.6 16.1 %copy-start.4 = (pred[640]{0:T(1024)(128)(4,1)S(1)}, pred[640]{0:T(1024)(128)(4,1)}, u32[]{:S(2)}) copy-start(pred[640]{0:T(1024)(128)(4,1)} %get-tuple-element.161) | copy-start | bytes 1924
  448.6 16.1 %copy-start.5 = (pred[640]{0:T(1024)(128)(4,1)S(1)}, pred[640]{0:T(1024)(128)(4,1)}, u32[]{:S(2)}) copy-start(pred[640]{0:T(1024)(128)(4,1)} %get-tuple-element.162) | copy-start | bytes 1924
  448.6 16.1 %copy-start.6 = (pred[640]{0:T(1024)(128)(4,1)S(1)}, pred[640]{0:T(1024)(128)(4,1)}, u32[]{:S(2)}) copy-start(pred[640]{0:T(1024)(128)(4,1)} %get-tuple-element.163) | copy-start | bytes 1924
  448.6 16.1 %copy-start.7 = (pred[640]{0:T(1024)(128)(4,1)S(1)}, pred[640]{0:T(1024)(128)(4,1)}, u32[]{:S(2)}) copy-start(pred[640]{0:T(1024)(128)(4,1)} %get-tuple-element.164) | copy-start | bytes 1924
  448.6 16.1 %copy-start.8 = (pred[640]{0:T(1024)(128)(4,1)S(1)}, pred[640]{0:T(1024)(128)(4,1)}, u32[]{:S(2)}) copy-start(pred[640]{0:T(1024)(128)(4,1)} %get-tuple-element.165) | copy-start | bytes 1924
  448.6 16.1 %copy-start.9 = (pred[640]{0:T(1024)(128)(4,1)S(1)}, pred[640]{0:T(1024)(128)(4,1)}, u32[]{:S(2)}) copy-start(pred[640]{0:T(1024)(128)(4,1)} %get-tuple-element.166) | copy-start | bytes 1924
  448.6 16.1 %copy-start.10 = (pred[640]{0:T(1024)(128)(4,1)S(1)}, pred[640]{0:T(1024)(128)(4,1)}, u32[]{:S(2)}) copy-start(pred[640]{0:T(1024)(128)(4,1)} %get-tuple-element.167) | copy-start | bytes 1924
  448.6 16.1 %copy-start.11 = (pred[640]{0:T(1024)(128)(4,1)S(1)}, pred[640]{0:T(1024)(128)(4,1)}, u32[]{:S(2)}) copy-start(pred[640]{0:T(1024)(128)(4,1)} %get-tuple-element.168) | copy-start | bytes 1924
  448.7 16.1 %copy-start.12 = (pred[640]{0:T(1024)(128)(4,1)S(1)}, pred[640]{0:T(1024)(128)(4,1)}, u32[]{:S(2)}) copy-start(pred[640]{0:T(1024)(128)(4,1)} %get-tuple-element.169) | copy-start | bytes 1924
  448.7 16.1 %copy-start.13 = (pred[640]{0:T(1024)(128)(4,1)S(1)}, pred[640]{0:T(1024)(128)(4,1)}, u32[]{:S(2)}) copy-start(pred[640]{0:T(1024)(128)(4,1)} %get-tuple-element.170) | copy-start | bytes 1924
  448.7 16.1 %copy-start.14 = (pred[640]{0:T(1024)(128)(4,1)S(1)}, pred[640]{0:T(1024)(128)(4,1)}, u32[]{:S(2)}) copy-start(pred[640]{0:T(1024)(128)(4,1)} %get-tuple-element.171) | copy-start | bytes 1924
  448.7 16.1 %copy-start.15 = (pred[640]{0:T(1024)(128)(4,1)S(1)}, pred[640]{0:T(1024)(128)(4,1)}, u32[]{:S(2)}) copy-start(pred[640]{0:T(1024)(128)(4,1)} %get-tuple-element.172) | copy-start | bytes 1924
  448.7 16.1 %copy-start.16 = (pred[640]{0:T(1024)(128)(4,1)S(1)}, pred[640]{0:T(1024)(128)(4,1)}, u32[]{:S(2)}) copy-start(pred[640]{0:T(1024)(128)(4,1)} %get-tuple-element.173) | copy-start | bytes 1924
  448.7 16.1 %copy-start.17 = (pred[640]{0:T(1024)(128)(4,1)S(1)}, pred[640]{0:T(1024)(128)(4,1)}, u32[]{:S(2)}) copy-start(pred[640]{0:T(1024)(128)(4,1)} %get-tuple-element.174) | copy-start | bytes 1924
  448.7 16.1 %copy-start.18 = (pred[640]{0:T(1024)(128)(4,1)S(1)}, pred[640]{0:T(1024)(128)(4,1)}, u32[]{:S(2)}) copy-start(pred[640]{0:T(1024)(128)(4,1)} %get-tuple-element.175) | copy-start | bytes 1924
  448.7 16.1 %copy-start.19 = (pred[640]{0:T(1024)(128)(4,1)S(1)}, pred[640]{0:T(1024)(128)(4,1)}, u32[]{:S(2)}) copy-start(pred[640]{0:T(1024)(128)(4,1)} %get-tuple-element.176) | copy-start | bytes 1924
  448.7 16.1 %copy-start.20 = (pred[640]{0:T(1024)(128)(4,1)S(1)}, pred[640]{0:T(1024)(128)(4,1)}, u32[]{:S(2)}) copy-start(pred[640]{0:T(1024)(128)(4,1)} %get-tuple-element.177) | copy-start | bytes 1924
  448.7 16.1 %copy-start.21 = (pred[640]{0:T(1024)(128)(4,1)S(1)}, pred[640]{0:T(1024)(128)(4,1)}, u32[]{:S(2)}) copy-start(pred[640]{0:T(1024)(128)(4,1)} %get-tuple-element.178) | copy-start | bytes 1924
  448.8 16.1 %copy-start.22 = (pred[640]{0:T(1024)(128)(4,1)S(1)}, pred[640]{0:T(1024)(128)(4,1)}, u32[]{:S(2)}) copy-start(pred[640]{0:T(1024)(128)(4,1)} %get-tuple-element.179) | copy-start | bytes 1924
  448.8 16.1 %copy-start.23 = (pred[640]{0:T(1024)(128)(4,1)S(1)}, pred[640]{0:T(1024)(128)(4,1)}, u32[]{:S(2)}) copy-start(pred[640]{0:T(1024)(128)(4,1)} %get-tuple-element.180) | copy-start | bytes 1924
  448.8 16.1 %copy-start.24 = (pred[640]{0:T(1024)(128)(4,1)S(1)}, pred[640]{0:T(1024)(128)(4,1)}, u32[]{:S(2)}) copy-start(pred[640]{0:T(1024)(128)(4,1)} %get-tuple-element.181) | copy-start | bytes 1924
  448.8 16.1 %copy-start.25 = (pred[640]{0:T(1024)(128)(4,1)S(1)}, pred[640]{0:T(1024)(128)(4,1)}, u32[]{:S(2)}) copy-start(pred[640]{0:T(1024)(128)(4,1)} %get-tuple-element.182) | copy-start | bytes 1924
  448.8 16.1 %copy-start.26 = (pred[640]{0:T(1024)(128)(4,1)S(1)}, pred[640]{0:T(1024)(128)(4,1)}, u32[]{:S(2)}) copy-start(pred[640]{0:T(1024)(128)(4,1)} %get-tuple-element.183) | copy-start | bytes 1924
  448.8 16.1 %copy-start.27 = (pred[640]{0:T(1024)(128)(4,1)S(1)}, pred[640]{0:T(1024)(128)(4,1)}, u32[]{:S(2)}) copy-start(pred[640]{0:T(1024)(128)(4,1)} %get-tuple-element.184) | copy-start | bytes 1924
  448.8 16.1 %copy-start.28 = (pred[640]{0:T(1024)(128)(4,1)S(1)}, pred[640]{0:T(1024)(128)(4,1)}, u32[]{:S(2)}) copy-start(pred[640]{0:T(1024)(128)(4,1)} %get-tuple-element.185) | copy-start | bytes 1924
  448.8 16.1 %copy-start.29 = (pred[640]{0:T(1024)(128)(4,1)S(1)}, pred[640]{0:T(1024)(128)(4,1)}, u32[]{:S(2)}) copy-start(pred[640]{0:T(1024)(128)(4,1)} %get-tuple-element.186) | copy-start | bytes 1924
  448.8 16.1 %copy-start.30 = (pred[640]{0:T(1024)(128)(4,1)S(1)}, pred[640]{0:T(1024)(128)(4,1)}, u32[]{:S(2)}) copy-start(pred[640]{0:T(1024)(128)(4,1)} %get-tuple-element.187) | copy-start | bytes 1924
  448.8 16.1 %copy-start.31 = (pred[640]{0:T(1024)(128)(4,1)S(1)}, pred[640]{0:T(1024)(128)(4,1)}, u32[]{:S(2)}) copy-start(pred[640]{0:T(1024)(128)(4,1)} %get-tuple-element.188) | copy-start | bytes 1924
  448.9 16.1 %copy-start.32 = (pred[640]{0:T(1024)(128)(4,1)S(1)}, pred[640]{0:T(1024)(128)(4,1)}, u32[]{:S(2)}) copy-start(pred[640]{0:T(1024)(128)(4,1)} %get-tuple-element.189) | copy-start | bytes 1924
  448.9 16.1 %copy-start.33 = (pred[640]{0:T(1024)(128)(4,1)S(1)}, pred[640]{0:T(1024)(128)(4,1)}, u32[]{:S(2)}) copy-start(pred[640]{0:T(1024)(128)(4,1)} %get-tuple-element.190) | copy-start | bytes 1924
  448.9 16.1 %copy-start.34 = (pred[640]{0:T(1024)(128)(4,1)S(1)}, pred[640]{0:T(1024)(128)(4,1)}, u32[]{:S(2)}) copy-start(pred[640]{0:T(1024)(128)(4,1)} %get-tuple-element.191) | copy-start | bytes 1924
  448.9 16.1 %copy-start.35 = (pred[640]{0:T(1024)(128)(4,1)S(1)}, pred[640]{0:T(1024)(128)(4,1)}, u32[]{:S(2)}) copy-start(pred[640]{0:T(1024)(128)(4,1)} %get-tuple-element.192) | copy-start | bytes 1924
  448.9 16.1 %copy-start.36 = (pred[640]{0:T(1024)(128)(4,1)S(1)}, pred[640]{0:T(1024)(128)(4,1)}, u32[]{:S(2)}) copy-start(pred[640]{0:T(1024)(128)(4,1)} %get-tuple-element.193) | copy-start | bytes 1924
  448.9 16.1 %copy-start.37 = (pred[640]{0:T(1024)(128)(4,1)S(1)}, pred[640]{0:T(1024)(128)(4,1)}, u32[]{:S(2)}) copy-start(pred[640]{0:T(1024)(128)(4,1)} %get-tuple-element.194) | copy-start | bytes 1924
  448.9 16.1 %copy-start.38 = (pred[640]{0:T(1024)(128)(4,1)S(1)}, pred[640]{0:T(1024)(128)(4,1)}, u32[]{:S(2)}) copy-start(pred[640]{0:T(1024)(128)(4,1)} %get-tuple-element.195) | copy-start | bytes 1924
  448.9 16.1 %copy-start.39 = (pred[640]{0:T(1024)(128)(4,1)S(1)}, pred[640]{0:T(1024)(128)(4,1)}, u32[]{:S(2)}) copy-start(pred[640]{0:T(1024)(128)(4,1)} %get-tuple-element.196) | copy-start | bytes 1924
  448.9 16.1 %copy-start.40 = (pred[640]{0:T(1024)(128)(4,1)S(1)}, pred[640]{0:T(1024)(128)(4,1)}, u32[]{:S(2)}) copy-start(pred[640]{0:T(1024)(128)(4,1)} %get-tuple-element.197) | copy-start | bytes 1924
  448.9 16.1 %copy-start.41 = (pred[640]{0:T(1024)(128)(4,1)S(1)}, pred[640]{0:T(1024)(128)(4,1)}, u32[]{:S(2)}) copy-start(pred[640]{0:T(1024)(128)(4,1)} %get-tuple-element.198) | copy-start | bytes 1924
  449.0 16.1 %copy-start.42 = (pred[640]{0:T(1024)(128)(4,1)S(1)}, pred[640]{0:T(1024)(128)(4,1)}, u32[]{:S(2)}) copy-start(pred[640]{0:T(1024)(128)(4,1)} %get-tuple-element.199) | copy-start | bytes 1924
  738.9 138.3 %copy-start = (bf16[640,1024]{1,0:T(8,128)(2,1)S(1)}, bf16[640,1024]{1,0:T(8,128)(2,1)}, u32[]{:S(2)}) copy-start(bf16[640,1024]{1,0:T(8,128)(2,1)} %param.7) | copy-start | bytes 3932164
Sparse Core Ops, SparseCore 0:
  9.1 383.6 all-gather.2
  394.6 336.7 all-gather.4
  739.0 138.1 reduce-scatter.1
